TPU v7x, 32 devices: a whole 2x2x4 slice. The times are simulated.
32 devices in a mesh: section: 4 (over y, x), mp: 2 (over core), dp: 4 (over z).
Axes of the slice: x: 2, y: 2, z: 4, core: 2. Of those that a mesh axis runs over, the one named last changes fastest.
Arguments:
- target_hidden: bfloat16 [4, 256, 8192], P('dp', None, 'section'), may hold values from -43 to 43, as said below
- embeds: bfloat16 [4, 256, 8192], P('dp', None, 'section'), may hold values from -50 to 50, as said below
- token_ids: int32 [4, 256], replicated, may hold values from 0 to 8191
- lengths: int32 [4], replicated, may hold values from 1 to 32, as said below
- offsets: int32 [4], replicated, may hold values from 0 to 224, as said below
- target_gain: float32 [8192], P('section'), may hold values from 0.5 to 1.5
- draft_gain: float32 [8192], P('section'), may hold values from 0.5 to 1.5
- head: bfloat16 [8192, 8192], P(('mp', 'dp'), 'section'), may hold values from -0.1875 to 0.1875
- fc_embed: bfloat16 [8192, 8192], P('section', ('mp', 'dp')), may hold values from -0.046875 to 0.046875
- fc_feature: bfloat16 [8192, 8192], P('section', ('mp', 'dp')), may hold values from -0.046875 to 0.046875
Outputs:
- loss: float32 [], replicated
- grad_embed: float32 [8192, 8192], P('section', ('mp', 'dp'))
- grad_feature: float32 [8192, 8192], P('section', ('mp', 'dp'))
Inputs may be any that keep to these rules, and one draw needn't show every extreme that they name: `lengths`: they sum to 64, and the longest response has exactly 32 rows. offsets + lengths <= 256 in every sequence; the sequence of the longest response starts at 224. `target_hidden`: real-valued features. `embeds`: real-valued embeddings.
All inputs are finite; a program needn't handle non-finite values.
Results may differ from a plain program's by a relative error of at most 0.0035.
The roundings to bfloat16 on the way count: a program that leaves them out, or rounds other values in their place, can miss the bound.
Values may be sent and summed in bfloat16 or wider, within the bound.
No kernel may reach another device: no remote copies, remote signals or barrier semaphores. Data moves between devices by JAX's collectives and lax.ppermute only.
A program may use at most 64 MiB of HBM per device.

v0:
```python
import jax
import jax.numpy as jnp
from jax import lax
from jax.sharding import PartitionSpec as P

D = 8192
R_OWN = 8
z_weight = 0.004
label_mix = 0.1
eps_norm = 1e-05


def contract_last(operand, weights):
    return lax.dot_general(
        operand, weights, (((1,), (1,)), ((), ())), preferred_element_type=jnp.float32
    )


def contract_first(operand, weights):
    return lax.dot_general(
        operand, weights, (((0,), (0,)), ((), ())), preferred_element_type=jnp.float32
    )


def sequence_of(packed, starts):
    return jnp.sum((starts[None, :] <= packed[:, None]).astype(jnp.int32), axis=1) - 1


def tile_sums(target_logit, draft_logit, labels, column_zero):
    is_label = (
        labels[:, None] - column_zero == jnp.arange(target_logit.shape[1], dtype=jnp.int32)[None, :]
    )
    target_exp = jnp.exp(target_logit)
    return (
        jnp.sum(target_exp, axis=1),
        jnp.sum(target_exp * draft_logit, axis=1),
        jnp.sum(jnp.exp(draft_logit), axis=1),
        jnp.sum(jnp.where(is_label, draft_logit, 0.0), axis=1),
    )


def tile_grad(target_logit, draft_logit, labels, column_zero, totals):
    target_total, cross_total, draft_total, label_logit = totals
    draft_lse = jnp.log(draft_total)
    target_lse = jnp.log(target_total)
    is_label = (
        labels[:, None] - column_zero == jnp.arange(target_logit.shape[1], dtype=jnp.int32)[None, :]
    )
    logit_grad = (
        (1.0 + 2.0 * z_weight * draft_lse)[:, None] * jnp.exp(draft_logit - draft_lse[:, None])
        - (1.0 - label_mix) * jnp.exp(target_logit - target_lse[:, None])
        - label_mix * is_label.astype(jnp.float32)
    )
    return logit_grad.astype(jnp.bfloat16)


def mean_loss(totals):
    target_total, cross_total, draft_total, label_logit = totals
    draft_lse = jnp.log(draft_total)
    row_loss = (
        draft_lse
        - (1.0 - label_mix) * cross_total / target_total
        - label_mix * label_logit
        + z_weight * draft_lse * draft_lse
    )
    return jnp.mean(row_loss)


def on_device(
    target_hidden,
    embeds,
    token_ids,
    lengths,
    offsets,
    target_gain,
    draft_gain,
    head,
    fc_embed,
    fc_feature,
):
    count_dp = lax.axis_size("dp")
    count_mp = lax.axis_size("mp")
    groups = count_mp * count_dp
    my_dp = lax.axis_index("dp")
    my_mp = lax.axis_index("mp")
    owner_index = my_mp * count_dp + my_dp
    section_index = lax.axis_index("section")
    slice_width = target_hidden.shape[2]
    seq_len = target_hidden.shape[1]
    vocab_tile = head.shape[0]
    slot_count = 2 * R_OWN // count_dp
    total_rows = R_OWN * groups
    starts = jnp.cumsum(lengths) - lengths
    first_row = starts[my_dp]
    my_count = lengths[my_dp]
    my_offset = offsets[my_dp]
    residue = my_mp * count_dp + jnp.arange(count_dp, dtype=jnp.int32)
    first_slot = (first_row - residue + groups - 1) // groups
    packed = (
        groups * (first_slot[:, None] + jnp.arange(slot_count, dtype=jnp.int32)[None, :])
        + residue[:, None]
    )
    is_live = (packed < first_row + my_count).reshape(-1, 1)
    flat_position = jnp.clip(my_offset + packed - first_row, 0, seq_len - 1).reshape(-1)
    taken_embed = jnp.take(embeds[0], flat_position, axis=0)
    taken_feature = jnp.take(target_hidden[0], flat_position, axis=0)
    send_embed = jnp.where(is_live, taken_embed, jnp.zeros_like(taken_embed)).reshape(
        count_dp, slot_count, slice_width
    )
    send_feature = jnp.where(is_live, taken_feature, jnp.zeros_like(taken_feature)).reshape(
        count_dp, slot_count, slice_width
    )
    got_embed, got_feature = (
        lax.all_to_all(send_embed, "dp", split_axis=0, concat_axis=0, tiled=True),
        lax.all_to_all(send_feature, "dp", split_axis=0, concat_axis=0, tiled=True),
    )
    slot_index = jnp.arange(R_OWN, dtype=jnp.int32)
    wanted = groups * slot_index + owner_index
    source = sequence_of(wanted, starts)
    source_first = (starts[source] - owner_index + groups - 1) // groups
    pick_index = source * slot_count + slot_index - source_first
    own_embed = jnp.take(got_embed.reshape(count_dp * slot_count, slice_width), pick_index, axis=0)
    own_feature = jnp.take(
        got_feature.reshape(count_dp * slot_count, slice_width), pick_index, axis=0
    )
    embed_all, feature_all = (
        lax.all_gather(own_embed, ("mp", "dp"), axis=0, tiled=True),
        lax.all_gather(own_feature, ("mp", "dp"), axis=0, tiled=True),
    )
    row_id = jnp.arange(total_rows, dtype=jnp.int32)
    packed_all = groups * (row_id % R_OWN) + row_id // R_OWN
    seq_all = sequence_of(packed_all, starts)
    position_all = offsets[seq_all] + packed_all - starts[seq_all]
    labels = token_ids.reshape(-1)[seq_all * seq_len + position_all]
    target_square = lax.psum(
        jnp.sum(jnp.square(feature_all.astype(jnp.float32)), axis=1), "section"
    )
    target_scale = lax.rsqrt(target_square / D + eps_norm)
    target_norm = (feature_all.astype(jnp.float32) * target_scale[:, None] * target_gain).astype(
        jnp.bfloat16
    )
    partial_value = jnp.dot(embed_all, fc_embed, preferred_element_type=jnp.float32) + jnp.dot(
        feature_all, fc_feature, preferred_element_type=jnp.float32
    )
    summed = lax.psum(partial_value, "section")
    spread = lax.all_to_all(summed, ("mp", "dp"), split_axis=0, concat_axis=1, tiled=True)
    hidden = lax.dynamic_slice_in_dim(spread, section_index * slice_width, slice_width, 1)
    draft_square = lax.psum(jnp.sum(hidden * hidden, axis=1), "section")
    draft_scale = lax.rsqrt(draft_square / D + eps_norm)
    draft_norm = (hidden * draft_scale[:, None] * draft_gain).astype(jnp.bfloat16)
    target_part = contract_last(target_norm, head)
    draft_part = contract_last(lax.all_gather(draft_norm, ("mp", "dp"), axis=0, tiled=True), head)
    target_logit, draft_logit = lax.psum((target_part, draft_part), "section")
    column_zero = owner_index * vocab_tile
    totals = lax.psum(tile_sums(target_logit, draft_logit, labels, column_zero), ("mp", "dp"))
    grad_tile = tile_grad(target_logit, draft_logit, labels, column_zero, totals)
    loss = mean_loss(totals)
    draft_grad = lax.psum_scatter(
        jnp.dot(grad_tile, head, preferred_element_type=jnp.float32),
        ("mp", "dp"),
        scatter_dimension=0,
        tiled=True,
    )
    upstream = draft_grad * draft_gain
    inner_sum = lax.psum(jnp.sum(hidden * upstream, axis=1), "section")
    hidden_grad = (
        draft_scale[:, None] * upstream - hidden * (draft_scale**3 * inner_sum / D)[:, None]
    ).astype(jnp.bfloat16)
    full_grad = lax.all_gather(hidden_grad, "section", axis=1, tiled=True)
    block_grad = lax.all_to_all(full_grad, ("mp", "dp"), split_axis=1, concat_axis=0, tiled=True)
    grad_embed = contract_first(embed_all, block_grad)
    grad_feature = contract_first(feature_all, block_grad)
    return (loss, grad_embed, grad_feature)


def solution(mesh):
    return jax.shard_map(
        on_device,
        mesh=mesh,
        in_specs=(
            P("dp", None, "section"),
            P("dp", None, "section"),
            P(),
            P(),
            P(),
            P("section"),
            P("section"),
            P(("mp", "dp"), "section"),
            P("section", ("mp", "dp")),
            P("section", ("mp", "dp")),
        ),
        out_specs=(P(), P("section", ("mp", "dp")), P("section", ("mp", "dp"))),
        check_vma=False,
    )
```

profile of v0, /device:TPU:0, one launch (start us, length us, event | category | flops | bytes accessed | tf_op | source)
XLA Modules:
  0.0 335.6 jit_solution(14348024160950690089)
XLA Ops:
  7.2 1.4 dynamic_slice.13
  10.1 1.5 fusion.37
  12.3 1.4 subtract_clamp_fusion
  15.9 2.0 gather_fusion.2
  18.6 6.3 %all-to-all-start.1 = ((bf16[4,4,2048]{2,1,0:T(4,128)(2,1)}), bf16[4,4,2048]{2,1,0:T(4,128)(2,1)S(1)}, u32[]{:S(2)}, u32[]{:S(2)}) async-start(bf16[4,4,2048]{2,1,0:T(4,128)(2,1)} %reshape.273), calls=%async_computation.1 | async-start | bytes 131072 | tf_op jit(solution)/shard_map/all_to_all | solution.py:115
  26.4 4.3 %all-to-all-done.1 = bf16[4,4,2048]{2,1,0:T(4,128)(2,1)S(1)} async-done(((bf16[4,4,2048]{2,1,0:T(4,128)(2,1)}), bf16[4,4,2048]{2,1,0:T(4,128)(2,1)S(1)}, u32[]{:S(2)}, u32[]{:S(2)}) %all-to-all-start.1) | async-done | bytes 65568 | tf_op jit(solution)/shard_map/all_to_all | solution.py:115
  30.7 3.3 all-to-all-start
  34.7 5.0 %all-to-all-done = bf16[4,4,2048]{2,1,0:T(4,128)(2,1)S(1)} async-done(((bf16[4,4,2048]{2,1,0:T(4,128)(2,1)}), bf16[4,4,2048]{2,1,0:T(4,128)(2,1)S(1)}, u32[]{:S(2)}, u32[]{:S(2)}) %all-to-all-start) | async-done | bytes 65568 | tf_op jit(solution)/shard_map/all_to_all | solution.py:114
  40.4 24.4 %all_gather.13 = bf16[64,2048]{1,0:T(8,128)(2,1)S(1)} all-gather(bf16[8,2048]{1,0:T(8,128)(2,1)S(1)} %get-tuple-element.35), channel_id=1, replica_groups=mesh['section'=4,'mp'=2,'dp'=4] {'mp','dp'}, dimensions={0}, use_global_device_ids=true | all-gather | bytes 294912 | tf_op jit(solution)/shard_map/all_gather | solution.py:128
  64.9 24.3 %all_gather.12 = bf16[64,2048]{1,0:T(8,128)(2,1)S(1)} all-gather(bf16[8,2048]{1,0:T(8,128)(2,1)S(1)} %get-tuple-element.36), channel_id=1, replica_groups=mesh['section'=4,'mp'=2,'dp'=4] {'mp','dp'}, dimensions={0}, use_global_device_ids=true | all-gather | bytes 294912 | tf_op jit(solution)/shard_map/all_gather | solution.py:127
  89.1 3.0 fusion.39
  92.2 1.6 fusion
  93.8 43.6 %all-reduce.6.cloned.1.call-done = f32[8,8,1024]{2,1,0:T(8,128)} async-done(((f32[8,8,1024]{2,1,0:T(8,128)}), f32[8,8,1024]{2,1,0:T(8,128)}) %all-reduce.6.cloned.1.call-update) | async-done | bytes 262160 | tf_op jit(solution)/shard_map/psum | solution.py:145
  137.4 4.6 %all-to-all-start.2 = ((f32[8,8,1024]{2,1,0:T(8,128)}), f32[8,8,1024]{2,1,0:T(8,128)S(1)}, u32[]{:S(2)}, u32[]{:S(2)}) async-start(f32[8,8,1024]{2,1,0:T(8,128)} %all-reduce.6.cloned.1.call-done), calls=%async_computation.2 | async-start | bytes 524288 | tf_op jit(solution)/shard_map/all_to_all | solution.py:146
  142.3 9.1 %all-to-all-done.2 = f32[8,8,1024]{2,1,0:T(8,128)S(1)} async-done(((f32[8,8,1024]{2,1,0:T(8,128)}), f32[8,8,1024]{2,1,0:T(8,128)S(1)}, u32[]{:S(2)}, u32[]{:S(2)}) %all-to-all-start.2) | async-done | bytes 262176 | tf_op jit(solution)/shard_map/all_to_all | solution.py:146
  151.5 8.9 %all-reduce.1 = (f32[8]{0:T(128)S(1)}, f32[64]{0:T(128)S(1)}) all-reduce(f32[8]{0:T(128)S(1)} %multiply_reduce_fusion.2, f32[64]{0:T(128)S(1)} %fusion.1), channel_id=1, replica_groups=mesh['section'=4,'mp'=2,'dp'=4] {'section'}, use_global_device_ids=true, to_apply=%region_4.7 | all-reduce | flops 72 | bytes 576 | tf_op jit(solution)/shard_map/psum | solution.py:148
  160.6 24.4 %all_gather.14 = bf16[64,2048]{1,0:T(8,128)(2,1)S(1)} all-gather(bf16[8,2048]{1,0:T(8,128)(2,1)S(1)} %multiply_convert_fusion), channel_id=1, replica_groups=mesh['section'=4,'mp'=2,'dp'=4] {'mp','dp'}, dimensions={0}, use_global_device_ids=true | all-gather | bytes 294912 | tf_op jit(solution)/shard_map/all_gather | solution.py:152
  185.0 4.3 %fusion.40 = f32[64,1024]{1,0:T(8,128)} fusion(bf16[64,2048]{1,0:T(8,128)(2,1)S(1)} %all_gather.14, bf16[1024,2048]{1,0:T(8,128)(2,1)} %param.21), kind=kOutput, calls=%fused_computation.111 | convolution fusion | flops 268435456 | bytes 4718592 | tf_op jit(solution)/shard_map/dot_general | solution.py:14
  189.3 2.1 fusion.4
  191.5 5.1 %fusion.31 = s32[64]{0:T(128)S(1)} fusion(s32[64]{0:T(128)S(1)} %convert_reduce_fusion, s32[]{:T(128)} %bitcast.19, s32[]{:T(128)} %bitcast.15, s32[]{:T(128)} %bitcast.20, s32[]{:T(128)} %bitcast.16, s32[]{:T(128)} %bitcast.22, s32[]{:T(128)} %bitcast.21, s32[]{:T(128)} %bitcast.18, s32[]{:T(128)} %bitcast.17), kind=kLoop, calls=%fused_computation.94 | loop fusion | flops 2176 | bytes 544 | tf_op jit(solution)/shard_map/select_n | solution.py:134
  197.3 37.7 %all-reduce.8.cloned.1.call-done = (f32[64,1024]{1,0:T(8,128)}, f32[64,1024]{1,0:T(8,128)}) async-done(((f32[64,1024]{1,0:T(8,128)}, f32[64,1024]{1,0:T(8,128)}), (f32[64,1024]{1,0:T(8,128)}, f32[64,1024]{1,0:T(8,128)})) %all-reduce.8.cloned.1.call-update) | async-done | bytes 524304 | tf_op jit(solution)/shard_map/psum | solution.py:153
  235.0 1.3 exponential_reduce_fusion
  236.3 15.9 %all-reduce = (f32[64]{0:T(128)S(1)}, f32[64]{0:T(128)S(1)}, f32[64]{0:T(128)S(1)}, f32[64]{0:T(128)S(1)}) all-reduce(f32[64]{0:T(128)S(1)} %get-tuple-element.6, f32[64]{0:T(128)S(1)} %get-tuple-element.8, f32[64]{0:T(128)S(1)} %get-tuple-element.7, f32[64]{0:T(128)S(1)} %get-tuple-element.5), channel_id=1, replica_groups=mesh['section'=4,'mp'=2,'dp'=4] {'mp','dp'}, use_global_device_ids=true, to_apply=%region_17.20 | all-reduce | flops 256 | bytes 2048 | tf_op jit(solution)/shard_map/psum | solution.py:155
  252.8 4.1 %fusion.8 = f32[64,2048]{1,0:T(8,128)} fusion(bf16[1024,2048]{1,0:T(8,128)(2,1)} %param.21, f32[64,1024]{1,0:T(8,128)} %get-tuple-element.16, f32[64,1024]{1,0:T(8,128)} %get-tuple-element.15, f32[64]{0:T(128)S(1)} %get-tuple-element.23, f32[64]{0:T(128)S(1)} %get-tuple-element.24, f32[64]{0:T(128)S(1)} %get-tuple-element.21, s32[64]{0:T(128)S(1)} %broadcast_subtract_fusion), kind=kOutput, calls=%fused_computation.22 | convolution fusion | flops 269025280 | bytes 5243904 | tf_op jit(solution)/shard_map/dot_general | solution.py:159
  257.0 31.1 %reduce-scatter.2.cloned.1.call-done = f32[8,2048]{1,0:T(8,128)} async-done(((f32[64,2048]{1,0:T(8,128)}), f32[8,2048]{1,0:T(8,128)}) %reduce-scatter.2.cloned.1.call-update) | async-done | bytes 65552 | tf_op jit(solution)/shard_map/reduce_scatter | solution.py:158
  288.1 1.0 multiply_reduce_fusion.1
  289.1 10.0 %psum.79 = f32[8]{0:T(128)S(1)} all-reduce(f32[8]{0:T(128)S(1)} %multiply_reduce_fusion.1), channel_id=1, replica_groups=mesh['section'=4,'mp'=2,'dp'=4] {'section'}, use_global_device_ids=true, to_apply=%region_21.24 | all-reduce | flops 8 | bytes 64 | tf_op jit(solution)/shard_map/psum | solution.py:165
  300.0 8.3 %all_gather.15 = bf16[8,8192]{1,0:T(8,128)(2,1)} all-gather(bf16[8,2048]{1,0:T(8,128)(2,1)S(1)} %subtract_convert_fusion.2), channel_id=1, replica_groups=mesh['section'=4,'mp'=2,'dp'=4] {'section'}, dimensions={1}, use_global_device_ids=true | all-gather | bytes 163840 | tf_op jit(solution)/shard_map/all_gather | solution.py:169
  308.3 3.4 %all-to-all-start.3 = ((bf16[8,8,1024]{2,0,1:T(8,128)(2,1)}), bf16[8,8,1024]{2,0,1:T(8,128)(2,1)S(1)}, u32[]{:S(2)}, u32[]{:S(2)}) async-start(bf16[8,8,1024]{2,0,1:T(8,128)(2,1)} %bitcast.24), calls=%async_computation.4 | async-start | bytes 262144 | tf_op jit(solution)/shard_map/all_to_all | solution.py:170
  312.3 6.2 %all-to-all-done.3 = bf16[8,8,1024]{2,0,1:T(8,128)(2,1)S(1)} async-done(((bf16[8,8,1024]{2,0,1:T(8,128)(2,1)}), bf16[8,8,1024]{2,0,1:T(8,128)(2,1)S(1)}, u32[]{:S(2)}, u32[]{:S(2)}) %all-to-all-start.3) | async-done | bytes 131104 | tf_op jit(solution)/shard_map/all_to_all | solution.py:170
  318.5 4.7 %fusion.9 = f32[2048,1024]{1,0:T(8,128)} fusion(bf16[64,2048]{1,0:T(8,128)(2,1)S(1)} %all_gather.13, bf16[8,8,1024]{2,0,1:T(8,128)(2,1)S(1)} %all-to-all-done.3), kind=kOutput, calls=%fused_computation.23 | convolution fusion | flops 268435456 | bytes 8781824 | tf_op jit(solution)/shard_map/dot_general | solution.py:20
  323.2 4.7 %fusion.11 = f32[2048,1024]{1,0:T(8,128)} fusion(bf16[64,2048]{1,0:T(8,128)(2,1)S(1)} %all_gather.12, bf16[8,8,1024]{2,0,1:T(8,128)(2,1)S(1)} %all-to-all-done.3), kind=kOutput, calls=%fused_computation.25 | convolution fusion | flops 268435456 | bytes 8781824 | tf_op jit(solution)/shard_map/dot_general | solution.py:20
  (58 shorter events, 9.4 us)
Async XLA Ops:
  7.2 8.1 %copy-start = (bf16[1,256,2048]{2,1,0:T(8,128)(2,1)S(1)}, bf16[1,256,2048]{2,1,0:T(8,128)(2,1)}, u32[]{:S(2)}) copy-start(bf16[1,256,2048]{2,1,0:T(8,128)(2,1)} %param.14) | copy-start | bytes 3145732
  18.6 12.1 %all-to-all-start.1 = ((bf16[4,4,2048]{2,1,0:T(4,128)(2,1)}), bf16[4,4,2048]{2,1,0:T(4,128)(2,1)S(1)}, u32[]{:S(2)}, u32[]{:S(2)}) async-start(bf16[4,4,2048]{2,1,0:T(4,128)(2,1)} %reshape.273), calls=%async_computation.1 | async-start | bytes 131072 | tf_op jit(solution)/shard_map/all_to_all | solution.py:115
  30.7 9.0 %all-to-all-start = ((bf16[4,4,2048]{2,1,0:T(4,128)(2,1)}), bf16[4,4,2048]{2,1,0:T(4,128)(2,1)S(1)}, u32[]{:S(2)}, u32[]{:S(2)}) async-start(bf16[4,4,2048]{2,1,0:T(4,128)(2,1)} %reshape.271), calls=%async_computation | async-start | bytes 131072 | tf_op jit(solution)/shard_map/all_to_all | solution.py:114
  34.0 103.4 %all-reduce.6.cloned.1.call-start = ((), (), s32[]{:S(2)}) async-start(), calls=%async_computation.5 | async-start | bytes 524288 | tf_op jit(solution)/shard_map/psum | solution.py:145
  40.3 51.8 %copy-start.2 = (bf16[2048,1024]{1,0:T(8,128)(2,1)S(1)}, bf16[2048,1024]{1,0:T(8,128)(2,1)}, u32[]{:S(2)}) copy-start(bf16[2048,1024]{1,0:T(8,128)(2,1)} %param.23) | copy-start | bytes 12582916
  92.2 59.3 %copy-start.5 = (s32[4,256]{1,0:T(4,128)S(1)}, s32[4,256]{1,0:T(4,128)}, u32[]{:S(2)}) copy-start(s32[4,256]{1,0:T(4,128)} %param.16) | copy-start | bytes 12292
  92.2 68.3 %copy-start.3 = (f32[2048]{0:T(1024)S(1)}, f32[2048]{0:T(1024)}, u32[]{:S(2)}) copy-start(f32[2048]{0:T(1024)} %param.20) | copy-start | bytes 24580
  93.7 95.5 %copy-start.4 = (f32[2048]{0:T(1024)S(1)}, f32[2048]{0:T(1024)}, u32[]{:S(2)}) copy-start(f32[2048]{0:T(1024)} %param.19) | copy-start | bytes 24580
  137.4 14.0 %all-to-all-start.2 = ((f32[8,8,1024]{2,1,0:T(8,128)}), f32[8,8,1024]{2,1,0:T(8,128)S(1)}, u32[]{:S(2)}, u32[]{:S(2)}) async-start(f32[8,8,1024]{2,1,0:T(8,128)} %all-reduce.6.cloned.1.call-done), calls=%async_computation.2 | async-start | bytes 524288 | tf_op jit(solution)/shard_map/all_to_all | solution.py:146
  142.0 93.0 %all-reduce.8.cloned.1.call-start = ((), (), s32[]{:S(2)}) async-start(), calls=%async_computation.7 | async-start | bytes 1048576 | tf_op jit(solution)/shard_map/psum | solution.py:153
  160.5 28.8 %copy-start.1 = (bf16[1024,2048]{1,0:T(8,128)(2,1)S(1)}, bf16[1024,2048]{1,0:T(8,128)(2,1)}, u32[]{:S(2)}) copy-start(bf16[1024,2048]{1,0:T(8,128)(2,1)} %param.21) | copy-start | bytes 12582916
  191.4 96.7 %reduce-scatter.2.cloned.1.call-start = ((), (), s32[]{:S(2)}) async-start(), calls=%async_computation.6 | async-start | bytes 589824 | tf_op jit(solution)/shard_map/reduce_scatter | solution.py:158
  308.3 10.2 %all-to-all-start.3 = ((bf16[8,8,1024]{2,0,1:T(8,128)(2,1)}), bf16[8,8,1024]{2,0,1:T(8,128)(2,1)S(1)}, u32[]{:S(2)}, u32[]{:S(2)}) async-start(bf16[8,8,1024]{2,0,1:T(8,128)(2,1)} %bitcast.24), calls=%async_computation.4 | async-start | bytes 262144 | tf_op jit(solution)/shard_map/all_to_all | solution.py:170
Sparse Core Ops, SparseCore 0:
  93.9 43.4 all-reduce.5
  191.6 43.4 all-reduce.7
  257.1 30.9 reduce-scatter.1
where the time goes:
time: 337 us; the launch traced here: 336 us
  waiting for transfers between devices  137 us (41%)
  blocking collectives  116 us (34%)
  matrix products  24.4 us (7%)
  starting transfers between devices  17.7 us (5%)
  between operations  17.1 us (5%)
  other arithmetic  13.2 us (4%)
  local copies, waits for them, and re-layouts  9.64 us (3%)
    psum x1, waiting for transfers between devices, on_device(): summed = lax.psum(partial_value, 'section')  43.6 us
    psum x1, waiting for transfers between devices, on_device(): target_logit, draft_logit = lax.psum((target_part, draft_part), 'section')  37.7 us
    reduce_scatter x1, waiting for transfers between devices, on_device(): lax.psum_scatter(jnp.dot(grad_tile, head, preferred_element_type=jnp.floa...  31.1 us
    all_gather x1, blocking collectives, on_device(): lax.all_gather(own_feature, ('mp', 'dp'), axis=0, tiled=True)  24.4 us
    all_gather x1, blocking collectives, on_device(): lax.all_gather(draft_norm, ('mp', 'dp'), axis=0, tiled=True)  24.4 us
    all_gather x1, blocking collectives, on_device(): lax.all_gather(own_embed, ('mp', 'dp'), axis=0, tiled=True)  24.3 us
    psum x1, blocking collectives, on_device(): lax.psum(tile_sums(target_logit, draft_logit, labels, column_zero), ('mp'...  15.9 us
    psum x1, blocking collectives, on_device(): inner_sum = lax.psum(jnp.sum(hidden * upstream, axis=1), 'section')  9.95 us
  transfers between devices with their start and end apart: 7, of which 7 were waited for; matrix products, arithmetic and copies ran while one was open for 2% of the time, Pallas kernels for 0%

commit v1 on v0

--- a/solution.py
+++ b/solution.py
@@ -8,6 +8,37 @@
 z_weight = 0.004
 label_mix = 0.1
 eps_norm = 1e-05
+
+
+def targets_search(view, dimension_no, buf):
+    raw_out, res = (view.shape[:dimension_no], view.shape[dimension_no + 1 :])
+    carry_out = jnp.moveaxis(view.reshape(*raw_out, buf, -1, *res), dimension_no, 0)
+    return carry_out
+
+
+def begin_the_sources_all(original, in_dim):
+    original = jnp.moveaxis(original, 0, in_dim)
+    e_now = original.shape
+    local_out = original.reshape(
+        *e_now[:in_dim], e_now[in_dim] * e_now[in_dim + 1], *e_now[in_dim + 2 :]
+    )
+    return local_out
+
+
+def direct_indices(inputs, peer_axis, inp, chunk):
+    arr_out = jax.lax.psum(1, axis_name=peer_axis)
+    view_out, r1 = (arr_out, jax.lax.axis_index(peer_axis))
+    v1 = targets_search(inputs, inp, view_out)
+    rows = [v1[r1]]
+    for ix in range(1, view_out):
+        answer = v1[r1 ^ ix]
+        v_now = jax.lax.ppermute(
+            answer, axis_name=peer_axis, perm=[(src_i, src_i ^ ix) for src_i in range(view_out)]
+        )
+        rows.append(v_now)
+    v1 = jnp.stack(rows, axis=0)[r1 ^ jnp.arange(view_out)]
+    arr_now = begin_the_sources_all(v1, chunk)
+    return arr_now
 
 
 def contract_last(operand, weights):
@@ -143,7 +174,7 @@
         feature_all, fc_feature, preferred_element_type=jnp.float32
     )
     summed = lax.psum(partial_value, "section")
-    spread = lax.all_to_all(summed, ("mp", "dp"), split_axis=0, concat_axis=1, tiled=True)
+    spread = direct_indices(summed, ("mp", "dp"), 0, 1)
     hidden = lax.dynamic_slice_in_dim(spread, section_index * slice_width, slice_width, 1)
     draft_square = lax.psum(jnp.sum(hidden * hidden, axis=1), "section")
     draft_scale = lax.rsqrt(draft_square / D + eps_norm)

time: 337 us -> 342 us (1.015)
  starting transfers between devices: 17.7 us -> 23.1 us
    ppermute x0 -> x7, starting transfers between devices: none -> 9.99 us  [direct_indices(): jax.lax.ppermute(answer, axis_name=peer_axis, perm=[(src_i, src_i ^ ix) f...]
    all_to_all x1 -> x0, waiting for transfers between devices: 9.06 us -> none  [on_device(): lax.all_to_all(summed, ('mp', 'dp'), split_axis=0, concat_axis=1, tiled=T...]
    ppermute x0 -> x7, waiting for transfers between devices: none -> 6.46 us  [direct_indices(): jax.lax.ppermute(answer, axis_name=peer_axis, perm=[(src_i, src_i ^ ix) f...]
    all_to_all x1 -> x0, starting transfers between devices: 4.61 us -> none  [on_device(): lax.all_to_all(summed, ('mp', 'dp'), split_axis=0, concat_axis=1, tiled=T...]
  transfers between devices with their start and end apart: 7 -> 13, of which waited for: 7 -> 8; matrix products, arithmetic and copies ran while one was open for 2% -> 2% of each run, Pallas kernels for 0% -> 0%
where the time goes in v1:
time: 342 us; the launch traced here: 341 us
  waiting for transfers between devices  135 us (39%)
  blocking collectives  116 us (34%)
  matrix products  24.4 us (7%)
  starting transfers between devices  23.1 us (7%)
  between operations  17.2 us (5%)
  other arithmetic  13.3 us (4%)
  local copies, waits for them, and re-layouts  11.1 us (3%)
    psum x1, waiting for transfers between devices, on_device(): summed = lax.psum(partial_value, 'section')  43.4 us
    psum x1, waiting for transfers between devices, on_device(): target_logit, draft_logit = lax.psum((target_part, draft_part), 'section')  38.9 us
    reduce_scatter x1, waiting for transfers between devices, on_device(): lax.psum_scatter(jnp.dot(grad_tile, head, preferred_element_type=jnp.floa...  31.1 us
    all_gather x1, blocking collectives, on_device(): lax.all_gather(draft_norm, ('mp', 'dp'), axis=0, tiled=True)  24.6 us
    all_gather x1, blocking collectives, on_device(): lax.all_gather(own_feature, ('mp', 'dp'), axis=0, tiled=True)  24.4 us
    all_gather x1, blocking collectives, on_device(): lax.all_gather(own_embed, ('mp', 'dp'), axis=0, tiled=True)  24.3 us
    psum x1, blocking collectives, on_device(): lax.psum(tile_sums(target_logit, draft_logit, labels, column_zero), ('mp'...  15.9 us
    ppermute x7, starting transfers between devices, direct_indices(): jax.lax.ppermute(answer, axis_name=peer_axis, perm=[(src_i, src_i ^ ix) f...  9.99 us
  transfers between devices with their start and end apart: 13, of which 8 were waited for; matrix products, arithmetic and copies ran while one was open for 2% of the time, Pallas kernels for 0%

profile of v1, /device:TPU:0, one launch (start us, length us, event | category | flops | bytes accessed | tf_op | source)
XLA Modules:
  0.0 341.0 jit_solution(17475907546098905689)
XLA Ops:
  10.1 1.5 fusion.38
  15.9 2.0 gather_fusion.3
  18.6 6.3 %all-to-all-start.1 = ((bf16[4,4,2048]{2,1,0:T(4,128)(2,1)}), bf16[4,4,2048]{2,1,0:T(4,128)(2,1)S(1)}, u32[]{:S(2)}, u32[]{:S(2)}) async-start(bf16[4,4,2048]{2,1,0:T(4,128)(2,1)} %reshape.292), calls=%async_computation.1 | async-start | bytes 131072 | tf_op jit(solution)/shard_map/all_to_all | solution.py:146
  26.4 4.3 %all-to-all-done.1 = bf16[4,4,2048]{2,1,0:T(4,128)(2,1)S(1)} async-done(((bf16[4,4,2048]{2,1,0:T(4,128)(2,1)}), bf16[4,4,2048]{2,1,0:T(4,128)(2,1)S(1)}, u32[]{:S(2)}, u32[]{:S(2)}) %all-to-all-start.1) | async-done | bytes 65568 | tf_op jit(solution)/shard_map/all_to_all | solution.py:146
  30.7 3.3 all-to-all-start
  34.7 5.0 %all-to-all-done = bf16[4,4,2048]{2,1,0:T(4,128)(2,1)S(1)} async-done(((bf16[4,4,2048]{2,1,0:T(4,128)(2,1)}), bf16[4,4,2048]{2,1,0:T(4,128)(2,1)S(1)}, u32[]{:S(2)}, u32[]{:S(2)}) %all-to-all-start) | async-done | bytes 65568 | tf_op jit(solution)/shard_map/all_to_all | solution.py:145
  40.4 24.4 %all_gather.13 = bf16[64,2048]{1,0:T(8,128)(2,1)S(1)} all-gather(bf16[8,2048]{1,0:T(8,128)(2,1)S(1)} %get-tuple-element.43), channel_id=1, replica_groups=mesh['section'=4,'mp'=2,'dp'=4] {'mp','dp'}, dimensions={0}, use_global_device_ids=true | all-gather | bytes 294912 | tf_op jit(solution)/shard_map/all_gather | solution.py:159
  64.9 24.3 %all_gather.12 = bf16[64,2048]{1,0:T(8,128)(2,1)S(1)} all-gather(bf16[8,2048]{1,0:T(8,128)(2,1)S(1)} %get-tuple-element.44), channel_id=1, replica_groups=mesh['section'=4,'mp'=2,'dp'=4] {'mp','dp'}, dimensions={0}, use_global_device_ids=true | all-gather | bytes 294912 | tf_op jit(solution)/shard_map/all_gather | solution.py:158
  89.1 3.0 fusion.40
  92.2 1.5 fusion
  94.0 43.4 %all-reduce.6.cloned.1.call-done = f32[8,8,1024]{2,1,0:T(8,128)} async-done(((f32[8,8,1024]{2,1,0:T(8,128)}), f32[8,8,1024]{2,1,0:T(8,128)}) %all-reduce.6.cloned.1.call-update) | async-done | bytes 262160 | tf_op jit(solution)/shard_map/psum | solution.py:176
  138.3 1.6 collective-permute-start
  142.9 1.4 collective-permute-start.3
  144.3 1.5 collective-permute-start.1
  145.8 3.4 collective-permute-done.1
  149.2 2.6 collective-permute-start.2
  151.9 3.1 collective-permute-done.2
  155.7 8.9 %all-reduce.1 = (f32[8]{0:T(128)S(1)}, f32[64]{0:T(128)S(1)}) all-reduce(f32[8]{0:T(128)S(1)} %multiply_reduce_fusion.2, f32[64]{0:T(128)S(1)} %fusion.1), channel_id=1, replica_groups=mesh['section'=4,'mp'=2,'dp'=4] {'section'}, use_global_device_ids=true, to_apply=%region_4.7 | all-reduce | flops 72 | bytes 576 | tf_op jit(solution)/shard_map/psum | solution.py:179
  164.8 24.6 %all_gather.14 = bf16[64,2048]{1,0:T(8,128)(2,1)S(1)} all-gather(bf16[8,2048]{1,0:T(8,128)(2,1)S(1)} %multiply_convert_fusion), channel_id=1, replica_groups=mesh['section'=4,'mp'=2,'dp'=4] {'mp','dp'}, dimensions={0}, use_global_device_ids=true | all-gather | bytes 294912 | tf_op jit(solution)/shard_map/all_gather | solution.py:183
  189.4 4.3 %fusion.41 = f32[64,1024]{1,0:T(8,128)} fusion(bf16[64,2048]{1,0:T(8,128)(2,1)S(1)} %all_gather.14, bf16[1024,2048]{1,0:T(8,128)(2,1)} %param.21), kind=kOutput, calls=%fused_computation.130 | convolution fusion | flops 268435456 | bytes 4718592 | tf_op jit(solution)/shard_map/dot_general | solution.py:45
  193.7 2.1 fusion.4
  195.9 5.1 %fusion.32 = s32[64]{0:T(128)S(1)} fusion(s32[64]{0:T(128)S(1)} %convert_reduce_fusion, s32[]{:T(128)} %bitcast.34, s32[]{:T(128)} %bitcast.30, s32[]{:T(128)} %bitcast.35, s32[]{:T(128)} %bitcast.31, s32[]{:T(128)} %bitcast.37, s32[]{:T(128)} %bitcast.36, s32[]{:T(128)} %bitcast.33, s32[]{:T(128)} %bitcast.32), kind=kLoop, calls=%fused_computation.113 | loop fusion | flops 2176 | bytes 544 | tf_op jit(solution)/shard_map/select_n | solution.py:165
  201.7 38.9 %all-reduce.8.cloned.1.call-done = (f32[64,1024]{1,0:T(8,128)}, f32[64,1024]{1,0:T(8,128)}) async-done(((f32[64,1024]{1,0:T(8,128)}, f32[64,1024]{1,0:T(8,128)}), (f32[64,1024]{1,0:T(8,128)}, f32[64,1024]{1,0:T(8,128)})) %all-reduce.8.cloned.1.call-update) | async-done | bytes 524304 | tf_op jit(solution)/shard_map/psum | solution.py:184
  241.8 15.9 %all-reduce = (f32[64]{0:T(128)S(1)}, f32[64]{0:T(128)S(1)}, f32[64]{0:T(128)S(1)}, f32[64]{0:T(128)S(1)}) all-reduce(f32[64]{0:T(128)S(1)} %get-tuple-element.6, f32[64]{0:T(128)S(1)} %get-tuple-element.8, f32[64]{0:T(128)S(1)} %get-tuple-element.7, f32[64]{0:T(128)S(1)} %get-tuple-element.5), channel_id=1, replica_groups=mesh['section'=4,'mp'=2,'dp'=4] {'mp','dp'}, use_global_device_ids=true, to_apply=%region_17.20 | all-reduce | flops 256 | bytes 2048 | tf_op jit(solution)/shard_map/psum | solution.py:186
  258.4 4.1 %fusion.8 = f32[64,2048]{1,0:T(8,128)} fusion(bf16[1024,2048]{1,0:T(8,128)(2,1)} %param.21, f32[64,1024]{1,0:T(8,128)} %get-tuple-element.16, f32[64,1024]{1,0:T(8,128)} %get-tuple-element.15, f32[64]{0:T(128)S(1)} %get-tuple-element.31, f32[64]{0:T(128)S(1)} %get-tuple-element.32, f32[64]{0:T(128)S(1)} %get-tuple-element.29, s32[64]{0:T(128)S(1)} %broadcast_subtract_fusion), kind=kOutput, calls=%fused_computation.23 | convolution fusion | flops 269025280 | bytes 5243904 | tf_op jit(solution)/shard_map/dot_general | solution.py:190
  262.5 31.1 %reduce-scatter.2.cloned.1.call-done = f32[8,2048]{1,0:T(8,128)} async-done(((f32[64,2048]{1,0:T(8,128)}), f32[8,2048]{1,0:T(8,128)}) %reduce-scatter.2.cloned.1.call-update) | async-done | bytes 65552 | tf_op jit(solution)/shard_map/reduce_scatter | solution.py:189
  294.6 9.9 %psum.79 = f32[8]{0:T(128)S(1)} all-reduce(f32[8]{0:T(128)S(1)} %multiply_reduce_fusion.1), channel_id=1, replica_groups=mesh['section'=4,'mp'=2,'dp'=4] {'section'}, use_global_device_ids=true, to_apply=%region_21.24 | all-reduce | flops 8 | bytes 64 | tf_op jit(solution)/shard_map/psum | solution.py:196
  305.4 8.3 %all_gather.15 = bf16[8,8192]{1,0:T(8,128)(2,1)} all-gather(bf16[8,2048]{1,0:T(8,128)(2,1)S(1)} %subtract_convert_fusion.2), channel_id=1, replica_groups=mesh['section'=4,'mp'=2,'dp'=4] {'section'}, dimensions={1}, use_global_device_ids=true | all-gather | bytes 163840 | tf_op jit(solution)/shard_map/all_gather | solution.py:200
  313.7 3.4 all-to-all-start.2
  317.8 6.2 %all-to-all-done.2 = bf16[8,8,1024]{2,0,1:T(8,128)(2,1)S(1)} async-done(((bf16[8,8,1024]{2,0,1:T(8,128)(2,1)}), bf16[8,8,1024]{2,0,1:T(8,128)(2,1)S(1)}, u32[]{:S(2)}, u32[]{:S(2)}) %all-to-all-start.2) | async-done | bytes 131104 | tf_op jit(solution)/shard_map/all_to_all | solution.py:201
  324.0 4.7 %fusion.9 = f32[2048,1024]{1,0:T(8,128)} fusion(bf16[64,2048]{1,0:T(8,128)(2,1)S(1)} %all_gather.13, bf16[8,8,1024]{2,0,1:T(8,128)(2,1)S(1)} %all-to-all-done.2), kind=kOutput, calls=%fused_computation.24 | convolution fusion | flops 268435456 | bytes 8781824 | tf_op jit(solution)/shard_map/dot_general | solution.py:51
  328.7 4.7 %fusion.11 = f32[2048,1024]{1,0:T(8,128)} fusion(bf16[64,2048]{1,0:T(8,128)(2,1)S(1)} %all_gather.12, bf16[8,8,1024]{2,0,1:T(8,128)(2,1)S(1)} %all-to-all-done.2), kind=kOutput, calls=%fused_computation.26 | convolution fusion | flops 268435456 | bytes 8781824 | tf_op jit(solution)/shard_map/dot_general | solution.py:51
  (81 shorter events, 18.8 us)
Async XLA Ops:
  7.2 8.1 %copy-start = (bf16[1,256,2048]{2,1,0:T(8,128)(2,1)S(1)}, bf16[1,256,2048]{2,1,0:T(8,128)(2,1)}, u32[]{:S(2)}) copy-start(bf16[1,256,2048]{2,1,0:T(8,128)(2,1)} %param.14) | copy-start | bytes 3145732
  18.6 12.1 %all-to-all-start.1 = ((bf16[4,4,2048]{2,1,0:T(4,128)(2,1)}), bf16[4,4,2048]{2,1,0:T(4,128)(2,1)S(1)}, u32[]{:S(2)}, u32[]{:S(2)}) async-start(bf16[4,4,2048]{2,1,0:T(4,128)(2,1)} %reshape.292), calls=%async_computation.1 | async-start | bytes 131072 | tf_op jit(solution)/shard_map/all_to_all | solution.py:146
  30.7 9.0 %all-to-all-start = ((bf16[4,4,2048]{2,1,0:T(4,128)(2,1)}), bf16[4,4,2048]{2,1,0:T(4,128)(2,1)S(1)}, u32[]{:S(2)}, u32[]{:S(2)}) async-start(bf16[4,4,2048]{2,1,0:T(4,128)(2,1)} %reshape.290), calls=%async_computation | async-start | bytes 131072 | tf_op jit(solution)/shard_map/all_to_all | solution.py:145
  34.0 103.4 %all-reduce.6.cloned.1.call-start = ((), (), s32[]{:S(2)}) async-start(), calls=%async_computation.4 | async-start | bytes 524288 | tf_op jit(solution)/shard_map/psum | solution.py:176
  40.3 51.8 %copy-start.2 = (bf16[2048,1024]{1,0:T(8,128)(2,1)S(1)}, bf16[2048,1024]{1,0:T(8,128)(2,1)}, u32[]{:S(2)}) copy-start(bf16[2048,1024]{1,0:T(8,128)(2,1)} %param.23) | copy-start | bytes 12582916
  92.2 63.5 %copy-start.5 = (s32[4,256]{1,0:T(4,128)S(1)}, s32[4,256]{1,0:T(4,128)}, u32[]{:S(2)}) copy-start(s32[4,256]{1,0:T(4,128)} %param.16) | copy-start | bytes 12292
  92.2 72.5 %copy-start.3 = (f32[2048]{0:T(1024)S(1)}, f32[2048]{0:T(1024)}, u32[]{:S(2)}) copy-start(f32[2048]{0:T(1024)} %param.20) | copy-start | bytes 24580
  93.7 99.9 %copy-start.4 = (f32[2048]{0:T(1024)S(1)}, f32[2048]{0:T(1024)}, u32[]{:S(2)}) copy-start(f32[2048]{0:T(1024)} %param.19) | copy-start | bytes 24580
  93.8 146.8 %all-reduce.8.cloned.1.call-start = ((), (), s32[]{:S(2)}) async-start(), calls=%async_computation.6 | async-start | bytes 1048576 | tf_op jit(solution)/shard_map/psum | solution.py:184
  138.3 6.0 %collective-permute-start = (f32[8,1024]{1,0:T(8,128)S(1)}, f32[8,1024]{1,0:T(8,128)S(1)}, u32[]{:S(2)}, u32[]{:S(2)}) collective-permute-start(f32[8,1024]{1,0:T(8,128)S(1)} %get-tuple-element.25), channel_id=1, source_target_pairs={{0,1},{1,0},{2,3},{3,2},{4,5},{5,4},{6,7},{7,6},{8,9},{9,8},{10,11... | collective-permute-start | bytes 98312 | tf_op jit(solution)/shard_map/ppermute | solution.py:35
  140.0 15.0 %collective-permute-start.6 = (f32[8,1024]{1,0:T(8,128)S(1)}, f32[8,1024]{1,0:T(8,128)S(1)}, u32[]{:S(2)}, u32[]{:S(2)}) collective-permute-start(f32[8,1024]{1,0:T(8,128)S(1)} %get-tuple-element.19), channel_id=1, source_target_pairs={{0,7},{1,6},{2,5},{3,4},{4,3},{5,2},{6,1},{7,0},{8,15},{9,14},{10,... | collective-permute-start | bytes 98312 | tf_op jit(solution)/shard_map/ppermute | solution.py:35
  141.2 13.8 %collective-permute-start.5 = (f32[8,1024]{1,0:T(8,128)S(1)}, f32[8,1024]{1,0:T(8,128)S(1)}, u32[]{:S(2)}, u32[]{:S(2)}) collective-permute-start(f32[8,1024]{1,0:T(8,128)S(1)} %get-tuple-element.20), channel_id=1, source_target_pairs={{0,6},{1,7},{2,4},{3,5},{4,2},{5,3},{6,0},{7,1},{8,14},{9,15},{10,... | collective-permute-start | bytes 98312 | tf_op jit(solution)/shard_map/ppermute | solution.py:35
  141.8 13.1 %collective-permute-start.4 = (f32[8,1024]{1,0:T(8,128)S(1)}, f32[8,1024]{1,0:T(8,128)S(1)}, u32[]{:S(2)}, u32[]{:S(2)}) collective-permute-start(f32[8,1024]{1,0:T(8,128)S(1)} %get-tuple-element.21), channel_id=1, source_target_pairs={{0,5},{1,4},{2,7},{3,6},{4,1},{5,0},{6,3},{7,2},{8,13},{9,12},{10,... | collective-permute-start | bytes 98312 | tf_op jit(solution)/shard_map/ppermute | solution.py:35
  142.9 12.1 %collective-permute-start.3 = (f32[8,1024]{1,0:T(8,128)S(1)}, f32[8,1024]{1,0:T(8,128)S(1)}, u32[]{:S(2)}, u32[]{:S(2)}) collective-permute-start(f32[8,1024]{1,0:T(8,128)S(1)} %get-tuple-element.22), channel_id=1, source_target_pairs={{0,4},{1,5},{2,6},{3,7},{4,0},{5,1},{6,2},{7,3},{8,12},{9,13},{10,... | collective-permute-start | bytes 98312 | tf_op jit(solution)/shard_map/ppermute | solution.py:35
  144.3 4.9 %collective-permute-start.1 = (f32[8,1024]{1,0:T(8,128)S(1)}, f32[8,1024]{1,0:T(8,128)S(1)}, u32[]{:S(2)}, u32[]{:S(2)}) collective-permute-start(f32[8,1024]{1,0:T(8,128)S(1)} %get-tuple-element.24), channel_id=1, source_target_pairs={{0,2},{1,3},{2,0},{3,1},{4,6},{5,7},{6,4},{7,5},{8,10},{9,11},{10,... | collective-permute-start | bytes 98312 | tf_op jit(solution)/shard_map/ppermute | solution.py:35
  149.2 5.7 %collective-permute-start.2 = (f32[8,1024]{1,0:T(8,128)S(1)}, f32[8,1024]{1,0:T(8,128)S(1)}, u32[]{:S(2)}, u32[]{:S(2)}) collective-permute-start(f32[8,1024]{1,0:T(8,128)S(1)} %get-tuple-element.23), channel_id=1, source_target_pairs={{0,3},{1,2},{2,1},{3,0},{4,7},{5,6},{6,5},{7,4},{8,11},{9,10},{10,... | collective-permute-start | bytes 98312 | tf_op jit(solution)/shard_map/ppermute | solution.py:35
  164.7 29.0 %copy-start.1 = (bf16[1024,2048]{1,0:T(8,128)(2,1)S(1)}, bf16[1024,2048]{1,0:T(8,128)(2,1)}, u32[]{:S(2)}) copy-start(bf16[1024,2048]{1,0:T(8,128)(2,1)} %param.21) | copy-start | bytes 12582916
  195.8 97.8 %reduce-scatter.2.cloned.1.call-start = ((), (), s32[]{:S(2)}) async-start(), calls=%async_computation.5 | async-start | bytes 589824 | tf_op jit(solution)/shard_map/reduce_scatter | solution.py:189
  313.7 10.2 %all-to-all-start.2 = ((bf16[8,8,1024]{2,0,1:T(8,128)(2,1)}), bf16[8,8,1024]{2,0,1:T(8,128)(2,1)S(1)}, u32[]{:S(2)}, u32[]{:S(2)}) async-start(bf16[8,8,1024]{2,0,1:T(8,128)(2,1)} %bitcast.39), calls=%async_computation.3 | async-start | bytes 262144 | tf_op jit(solution)/shard_map/all_to_all | solution.py:201
Sparse Core Ops, SparseCore 0:
  93.9 43.4 all-reduce.5
  195.9 44.5 all-reduce.7
  262.6 30.9 reduce-scatter.1
